TPU v7x, 32 devices: a whole 2x2x4 slice. The times are simulated.
32 devices in a mesh: grp: 2 (over y), row: 8 (over z, x), chan: 2 (over core).
Axes of the slice: x: 2, y: 2, z: 4, core: 2. Of those that a mesh axis runs over, the one named last changes fastest.
Arguments:
- band_strip: bfloat16 [424, 64, 128], P('chan', ('grp', 'row')), parts along dimension 1, may hold values from -6 to 6
- conv_weight: bfloat16 [1024, 9, 424], P('row', None, 'chan'), may hold values from -0.09375 to 0.09375
- gdn_gamma: bfloat16 [1024, 1024], P('chan'), as said below
- gdn_beta: float32 [1024], P('chan'), may hold values from 0.5 to 2
- cotangent: bfloat16 [1024, 64, 128], P('chan', ('grp', 'row')), parts along dimension 1, may hold values from -6 to 6
Outputs:
- latent: bfloat16 [1024, 64, 128], P('chan', ('grp', 'row')), parts along dimension 1
- grad_strip: float32 [424, 64, 128], P('chan', ('grp', 'row')), parts along dimension 1
- grad_gamma: float32 [2048, 1024], P(('grp', 'chan')), parts along dimension 0
- grad_beta: float32 [2048], P(('grp', 'chan')), parts along dimension 0
There are 2 independent parts, one for each index of `grp`. A program takes and returns all parts, laid end to end along the dimension named above; an argument that names none is the same for every part. Nothing has to cross between parts.
Inputs may be any that keep to these rules, and one draw needn't show every extreme that they name: `gdn_gamma`: gamma's entries are non-negative.
All inputs are finite; a program needn't handle non-finite values.
Results may differ from a plain program's by a relative error of at most 0.0054.
Values may be sent and summed in bfloat16 or wider, within the bound.
No kernel may reach another device: no remote copies, remote signals or barrier semaphores. Data moves between devices by JAX's collectives and lax.ppermute only.
A program may use at most 64 MiB of HBM per device.

v0:
```python
import math
import jax
import jax.numpy as jnp
from jax import lax
from jax.sharding import PartitionSpec as P

TAPS = ((-1, -1), (-1, 0), (-1, 1), (0, -1), (0, 0), (0, 1), (1, -1), (1, 0), (1, 1))


def extended(shard, sides, width):
    for axis, dim in sides:
        count, length = (lax.axis_size(axis), shard.shape[dim])
        up = [(i, (i + 1) % count) for i in range(count - 1)]
        down = [(j, i) for i, j in up]
        last = lax.slice_in_dim(shard, length - width, length, axis=dim)
        leading = lax.slice_in_dim(shard, 0, width, axis=dim)
        before = lax.ppermute(last, axis, up)
        after = lax.ppermute(leading, axis, down)
        shard = jnp.concatenate([before, shard, after], axis=dim)
    return shard


def tap_columns(rimmed, row_count, col_count):
    padded = jnp.pad(rimmed, ((0, 0), (0, 0), (1, 1)))
    stacked = jnp.stack(
        [
            padded[
                :,
                1 + row_shift : 1 + row_shift + row_count,
                1 + col_shift : 1 + col_shift + col_count,
            ]
            for row_shift, col_shift in TAPS
        ],
        axis=0,
    )
    return stacked.reshape(9 * rimmed.shape[0], row_count * col_count)


def per_device(band_strip, conv_weight, gdn_gamma, gdn_beta, cotangent):
    in_local = band_strip.shape[0]
    row_count = band_strip.shape[1]
    col_count = band_strip.shape[2]
    pixels = row_count * col_count
    lat_local = gdn_gamma.shape[0]
    rimmed = extended(band_strip, (("row", 1),), 1)
    columns = tap_columns(rimmed, row_count, col_count)
    shard_piece = lax.all_gather(conv_weight, "row", axis=0, tiled=True)
    flat = shard_piece.reshape(shard_piece.shape[0], 9 * in_local)
    partial_value = jnp.dot(flat, columns, preferred_element_type=jnp.float32)
    pre = lax.psum_scatter(partial_value, "chan", scatter_dimension=0, tiled=True)
    squares_own = (pre * pre).astype(jnp.bfloat16)
    squares = lax.all_gather(squares_own, "chan", axis=0, tiled=True)
    norm_value = gdn_beta[:, None] + jnp.dot(gdn_gamma, squares, preferred_element_type=jnp.float32)
    inverse = lax.rsqrt(norm_value)
    latent = (pre * inverse).astype(jnp.bfloat16)
    upstream = cotangent.reshape(lat_local, pixels).astype(jnp.float32)
    shares = (-0.5 * upstream * pre * inverse * inverse * inverse).astype(jnp.bfloat16)
    gamma_cols = lax.all_to_all(gdn_gamma, "chan", split_axis=1, concat_axis=0, tiled=True)
    shares_all = lax.all_gather(shares, "chan", axis=0, tiled=True)
    back_sum = lax.dot_general(
        gamma_cols, shares_all, (((0,), (0,)), ((), ())), preferred_element_type=jnp.float32
    )
    latent_grad = (upstream * inverse + 2.0 * pre * back_sum).astype(jnp.bfloat16)
    gamma_terms = lax.dot_general(
        shares, squares, (((1,), (1,)), ((), ())), preferred_element_type=jnp.float32
    )
    beta_terms = jnp.sum(shares.astype(jnp.float32), axis=1)
    gamma_total, beta_total = lax.psum((gamma_terms, beta_terms), "row")
    scale_factor = 1.0 / math.sqrt(pixels * lax.axis_size("row"))
    grad_gamma = gamma_total * scale_factor
    grad_beta = beta_total * scale_factor
    grad_all = lax.all_gather(
        latent_grad.reshape(lat_local, row_count, col_count), "chan", axis=0, tiled=True
    )
    grad_rimmed = extended(grad_all, (("row", 1),), 1)
    grad_padded = jnp.pad(grad_rimmed, ((0, 0), (0, 0), (1, 1)))
    initial = jnp.zeros((in_local, pixels), jnp.float32)
    running = initial
    shard_piece = lax.all_gather(conv_weight, "row", axis=0, tiled=True)
    count_rows = shard_piece.shape[0]
    for tap_index, (row_shift, col_shift) in enumerate(TAPS):
        window = grad_padded[
            :, 1 - row_shift : 1 - row_shift + row_count, 1 - col_shift : 1 - col_shift + col_count
        ].reshape(count_rows, pixels)
        running = running + lax.dot_general(
            shard_piece[:, tap_index, :],
            window,
            (((0,), (0,)), ((), ())),
            preferred_element_type=jnp.float32,
        )
    return (
        latent.reshape(lat_local, row_count, col_count),
        running.reshape(in_local, row_count, col_count),
        grad_gamma,
        grad_beta,
    )


def solution(mesh):
    return jax.shard_map(
        per_device,
        mesh=mesh,
        in_specs=(
            P("chan", ("grp", "row"), None),
            P("row", None, "chan"),
            P("chan", None),
            P("chan"),
            P("chan", ("grp", "row"), None),
        ),
        out_specs=(
            P("chan", ("grp", "row"), None),
            P("chan", ("grp", "row"), None),
            P(("grp", "chan"), None),
            P(("grp", "chan")),
        ),
        check_vma=False,
    )
```

profile of v0, /device:TPU:0, one launch (start us, length us, event | category | flops | bytes accessed | tf_op | source)
XLA Modules:
  0.0 275.5 jit_solution(17126695772306795772)
XLA Ops:
  7.2 0.0 all-gather.5.cloned.1.call-start
  7.2 0.7 all-gather.5.cloned.1.call-update
  7.9 0.0 reduce-scatter.2.cloned.1.call-start
  8.0 1.2 fusion.48
  9.2 1.3 collective-permute-start.1
  10.5 5.5 %collective-permute-start = (bf16[212,1,128]{2,1,0:T(2,128)(2,1)S(1)}, bf16[212,1,128]{2,1,0:T(2,128)(2,1)S(1)}, u32[]{:S(2)}, u32[]{:S(2)}) collective-permute-start(bf16[212,1,128]{2,1,0:T(2,128)(2,1)S(1)} %get-tuple-element.30), channel_id=1, source_target_pairs={{0,2},{2,4},{4,6},{6,8},{8,10},{10,12},{12,14},{1,3},{3,5},{5,7},{... | collective-permute-start | bytes 162824 | tf_op jit(solution)/shard_map/ppermute | solution.py:17
  16.0 1.1 collective-permute-done.1
  17.1 2.5 collective-permute-done
  19.5 2.1 fusion.22
  21.6 0.1 fusion.44
  21.7 0.3 fusion.43
  22.0 0.3 fusion.41
  22.2 0.1 fusion.40
  22.4 0.1 bitcast_dynamic-update-slice_fusion
  22.5 0.4 fusion.39
  22.8 0.1 fusion.38
  23.0 0.3 fusion.37
  23.3 0.4 fusion.35
  23.6 0.8 pad.38
  24.5 0.3 copy.17
  24.8 60.2 %all-gather.5.cloned.1.call-done = bf16[1024,9,212]{0,2,1:T(8,128)(2,1)} async-done(((bf16[128,9,212]{0,2,1:T(8,128)(2,1)}), bf16[1024,9,212]{0,2,1:T(8,128)(2,1)}) %all-gather.5.cloned.1.call-update) | async-done | bytes 3907600 | tf_op jit(solution)/shard_map/all_gather | solution.py:47
  85.0 5.5 %reshape.58 = bf16[1024,1908]{0,1:T(8,128)(2,1)} reshape(bf16[1024,9,212]{0,2,1:T(8,128)(2,1)} %all-gather.5.cloned.1.call-done) | data formatting | bytes 7815168 | tf_op jit(solution)/shard_map/reshape | solution.py:48
  90.5 5.8 %convolution_bitcast_fusion = f32[1024,512]{0,1:T(8,128)} fusion(bf16[1908,512]{1,0:T(8,128)(2,1)S(1)} %bitcast.144, bf16[1024,1908]{0,1:T(8,128)(2,1)} %reshape.58), kind=kOutput, calls=%fused_computation.11 | convolution fusion | flops 2000683008 | bytes 7958528 | tf_op jit(solution)/shard_map/dot_general | solution.py:49
  96.3 0.0 reduce-scatter.2.cloned.1.call-update
  96.4 0.0 all-gather.7.cloned.1.call-start
  96.4 7.9 %reduce-scatter.2.cloned.1.call-done = f32[512,512]{0,1:T(8,128)} async-done(((f32[1024,512]{0,1:T(8,128)}), f32[512,512]{0,1:T(8,128)}) %reduce-scatter.2.cloned.1.call-update) | async-done | bytes 1048592 | tf_op jit(solution)/shard_map/reduce_scatter | solution.py:50
  104.3 2.2 multiply_convert_fusion.1
  106.5 0.0 all-gather.7.cloned.1.call-update
  106.6 0.0 all-gather.9.cloned.1.call-start
  106.6 1.4 copy.13
  108.0 9.0 %all-gather.7.cloned.1.call-done = bf16[1024,512]{0,1:T(8,128)(2,1)} async-done(((bf16[512,512]{0,1:T(8,128)(2,1)}), bf16[1024,512]{0,1:T(8,128)(2,1)}) %all-gather.7.cloned.1.call-update) | async-done | bytes 1048592 | tf_op jit(solution)/shard_map/all_gather | solution.py:52
  117.0 3.5 %convert_reduce_fusion = (f32[512]{0:T(512)S(1)}, bf16[512,512]{0,1:T(8,128)(2,1)}, f32[512,512]{0,1:T(8,128)}, bf16[512,512]{0,1:T(8,128)(2,1)}) fusion(f32[512,512]{0,1:T(8,128)S(1)} %copy-done.2, f32[512,4,128]{0,2,1:T(8,128)S(1)} %copy.13, bf16[1024,512]{0,1:T(8,128)(2,1)} %all-gather.7.cloned.1.call-done, bf16[512,1024]{1,0:T(8,128)(2,1)S(1)} %copy-done.6, ...), kind=kOutput, calls=%fused_computation.31 | convolution fusion | flops 540016128 | bytes 6295552 | tf_op jit(solution)/shard_map/dot_general | solution.py:53
  120.5 0.0 all-gather.9.cloned.1.call-update
  120.6 0.0 all-gather.11.cloned.1.call-start
  120.6 0.5 copy.14
  121.2 4.6 %all_to_all.19 = bf16[512,2,512]{0,2,1:T(8,128)(2,1)S(1)} all-to-all(bf16[512,2,512]{0,2,1:T(8,128)(2,1)S(1)} %bitcast.139), channel_id=1, replica_groups=mesh['grp'=2,'row'=8,'chan'=2] {'chan'}, dimensions={1} | all-to-all | bytes 2097152 | tf_op jit(solution)/shard_map/all_to_all | solution.py:58
  125.7 1.3 copy.15
  127.1 3.9 %all-gather.9.cloned.1.call-done = bf16[1024,512]{0,1:T(8,128)(2,1)} async-done(((bf16[512,512]{0,1:T(8,128)(2,1)}), bf16[1024,512]{0,1:T(8,128)(2,1)}) %all-gather.9.cloned.1.call-update) | async-done | bytes 1048592 | tf_op jit(solution)/shard_map/all_gather | solution.py:59
  130.9 3.5 %fusion.11 = bf16[512,512]{0,1:T(8,128)(2,1)} fusion(f32[512,512]{0,1:T(8,128)} %get-tuple-element.18, bf16[1024,512]{0,1:T(8,128)(2,1)} %all-gather.9.cloned.1.call-done, bf16[1024,512]{1,0:T(8,128)(2,1)} %bitcast.140, f32[512,512]{0,1:T(8,128)S(1)} %copy-done.2), kind=kOutput, calls=%fused_computation.19 | convolution fusion | flops 537919488 | bytes 4718592 | tf_op jit(solution)/shard_map/dot_general | solution.py:60
  134.5 0.0 all-gather.11.cloned.1.call-update
  134.5 0.0 all-reduce.4.cloned.1.call-start
  134.6 2.0 fusion.49
  136.6 1.0 copy-done.7
  137.6 1.1 copy.16
  138.7 21.8 %psum.15 = f32[512]{0:T(512)S(1)} all-reduce(f32[512]{0:T(512)S(1)} %get-tuple-element.16), channel_id=1, replica_groups=mesh['grp'=2,'row'=8,'chan'=2] {'row'}, use_global_device_ids=true, to_apply=%region_3.4 | all-reduce | flops 512 | bytes 4096 | tf_op jit(solution)/shard_map/psum | solution.py:68
  160.5 0.6 broadcast_multiply_fusion.1
  161.1 1.2 fusion.47
  162.3 1.3 collective-permute-start.3
  163.6 4.7 %collective-permute-start.2 = (bf16[1024,1,128]{0,2,1:T(8,128)(2,1)S(1)}, bf16[1024,1,128]{0,2,1:T(8,128)(2,1)S(1)}, u32[]{:S(2)}, u32[]{:S(2)}) collective-permute-start(bf16[1024,1,128]{0,2,1:T(8,128)(2,1)S(1)} %get-tuple-element.28), channel_id=1, source_target_pairs={{0,2},{2,4},{4,6},{6,8},{8,10},{10,12},{12,14},{1,3},{3,5},{5,7},{... | collective-permute-start | bytes 786440 | tf_op jit(solution)/shard_map/ppermute | solution.py:17
  168.3 89.7 %all-reduce.4.cloned.1.call-done = f32[512,1024]{1,0:T(8,128)} async-done(((f32[512,1024]{1,0:T(8,128)}), f32[512,1024]{1,0:T(8,128)}) %all-reduce.4.cloned.1.call-update) | async-done | bytes 2097168 | tf_op jit(solution)/shard_map/psum | solution.py:68
  258.0 3.4 %broadcast_multiply_fusion = f32[512,1024]{1,0:T(8,128)} fusion(f32[512,1024]{1,0:T(8,128)} %all-reduce.4.cloned.1.call-done), kind=kLoop, calls=%fused_computation.32 | loop fusion | flops 524288 | bytes 4194304 | tf_op jit(solution)/shard_map/mul | solution.py:70
  261.4 0.5 fusion.26
  261.9 0.5 fusion.6
  262.4 1.1 fusion.46
  263.5 0.2 pad_maximum_fusion.1
  263.7 0.5 fusion.23
  264.2 0.5 fusion.24
  264.7 0.5 fusion.25
  265.2 0.5 fusion.27
  265.7 0.5 fusion.28
  266.2 0.5 fusion.29
  266.7 0.5 fusion.34
  267.2 0.5 fusion.15
  267.8 0.9 reshape.70
  (21 shorter events, 0.1 us)
Async XLA Ops:
  7.2 14.6 %copy-start.3 = (bf16[212,4,128]{2,1,0:T(4,128)(2,1)S(1)}, bf16[212,4,128]{2,1,0:T(4,128)(2,1)}, u32[]{:S(2)}) copy-start(bf16[212,4,128]{2,1,0:T(4,128)(2,1)} %param.5) | copy-start | bytes 651268
  7.2 77.8 %all-gather.5.cloned.1.call-start = ((), (), s32[]{:S(2)}) async-start(), calls=%async_computation.2 | async-start | bytes 4478976 | tf_op jit(solution)/shard_map/all_gather | solution.py:47
  7.9 96.4 %reduce-scatter.2.cloned.1.call-start = ((), (), s32[]{:S(2)}) async-start(), calls=%async_computation.3 | async-start | bytes 3145728 | tf_op jit(solution)/shard_map/reduce_scatter | solution.py:50
  9.2 7.9 %collective-permute-start.1 = (bf16[212,1,128]{2,1,0:T(2,128)(2,1)S(1)}, bf16[212,1,128]{2,1,0:T(2,128)(2,1)S(1)}, u32[]{:S(2)}, u32[]{:S(2)}) collective-permute-start(bf16[212,1,128]{2,1,0:T(2,128)(2,1)S(1)} %get-tuple-element.31), channel_id=1, source_target_pairs={{2,0},{4,2},{6,4},{8,6},{10,8},{12,10},{14,12},{3,1},{5,3},{7,5},{... | collective-permute-start | bytes 162824 | tf_op jit(solution)/shard_map/ppermute | solution.py:18
  10.5 9.1 %collective-permute-start = (bf16[212,1,128]{2,1,0:T(2,128)(2,1)S(1)}, bf16[212,1,128]{2,1,0:T(2,128)(2,1)S(1)}, u32[]{:S(2)}, u32[]{:S(2)}) collective-permute-start(bf16[212,1,128]{2,1,0:T(2,128)(2,1)S(1)} %get-tuple-element.30), channel_id=1, source_target_pairs={{0,2},{2,4},{4,6},{6,8},{8,10},{10,12},{12,14},{1,3},{3,5},{5,7},{... | collective-permute-start | bytes 162824 | tf_op jit(solution)/shard_map/ppermute | solution.py:17
  96.3 20.7 %copy-start.6 = (bf16[512,1024]{1,0:T(8,128)(2,1)S(1)}, bf16[512,1024]{1,0:T(8,128)(2,1)}, u32[]{:S(2)}) copy-start(bf16[512,1024]{1,0:T(8,128)(2,1)} %param.7) | copy-start | bytes 3145732
  96.4 20.7 %copy-start.8 = (f32[512]{0:T(512)S(1)}, f32[512]{0:T(512)}, u32[]{:S(2)}) copy-start(f32[512]{0:T(512)} %param.8) | copy-start | bytes 6148
  96.4 20.6 %all-gather.7.cloned.1.call-start = ((), (), s32[]{:S(2)}) async-start(), calls=%async_computation.4 | async-start | bytes 1572864 | tf_op jit(solution)/shard_map/all_gather | solution.py:52
  104.3 12.7 %copy-start.2 = (f32[512,512]{0,1:T(8,128)S(1)}, f32[512,512]{0,1:T(8,128)}, u32[]{:S(2)}) copy-start(f32[512,512]{0,1:T(8,128)} %reduce-scatter.2.cloned.1.call-done) | copy-start | bytes 3145732
  106.6 24.4 %all-gather.9.cloned.1.call-start = ((), (), s32[]{:S(2)}) async-start(), calls=%async_computation.5 | async-start | bytes 1572864 | tf_op jit(solution)/shard_map/all_gather | solution.py:59
  120.6 40.5 %all-gather.11.cloned.1.call-start = ((), (), s32[]{:S(2)}) async-start(), calls=%async_computation.6 | async-start | bytes 1572864 | tf_op jit(solution)/shard_map/all_gather | solution.py:72
  130.9 3.6 %copy-start.4 = (bf16[512,512]{0,1:T(8,128)(2,1)S(1)}, bf16[512,512]{0,1:T(8,128)(2,1)}, u32[]{:S(2)}) copy-start(bf16[512,512]{0,1:T(8,128)(2,1)} %get-tuple-element.17) | copy-start | bytes 1572868
  130.9 3.6 %copy-start.5 = (bf16[1024,512]{0,1:T(8,128)(2,1)S(1)}, bf16[1024,512]{0,1:T(8,128)(2,1)}, u32[]{:S(2)}) copy-start(bf16[1024,512]{0,1:T(8,128)(2,1)} %all-gather.7.cloned.1.call-done) | copy-start | bytes 3145732
  134.5 123.5 %all-reduce.4.cloned.1.call-start = ((), (), s32[]{:S(2)}) async-start(), calls=%async_computation.7 | async-start | bytes 4194304 | tf_op jit(solution)/shard_map/psum | solution.py:68
  136.6 1.0 copy-start.7
  161.1 100.2 %copy-start.1 = (bf16[1024,4,128]{0,2,1:T(8,128)(2,1)S(1)}, bf16[1024,4,128]{0,2,1:T(8,128)(2,1)}, u32[]{:S(2)}) copy-start(bf16[1024,4,128]{0,2,1:T(8,128)(2,1)} %all-gather.11.cloned.1.call-done) | copy-start | bytes 3145732
  162.3 99.6 %collective-permute-start.3 = (bf16[1024,1,128]{0,2,1:T(8,128)(2,1)S(1)}, bf16[1024,1,128]{0,2,1:T(8,128)(2,1)S(1)}, u32[]{:S(2)}, u32[]{:S(2)}) collective-permute-start(bf16[1024,1,128]{0,2,1:T(8,128)(2,1)S(1)} %get-tuple-element.29), channel_id=1, source_target_pairs={{2,0},{4,2},{6,4},{8,6},{10,8},{12,10},{14,12},{3,1},{5,3},{7,5},{... | collective-permute-start | bytes 786440 | tf_op jit(solution)/shard_map/ppermute | solution.py:18
  163.6 98.3 %collective-permute-start.2 = (bf16[1024,1,128]{0,2,1:T(8,128)(2,1)S(1)}, bf16[1024,1,128]{0,2,1:T(8,128)(2,1)S(1)}, u32[]{:S(2)}, u32[]{:S(2)}) collective-permute-start(bf16[1024,1,128]{0,2,1:T(8,128)(2,1)S(1)} %get-tuple-element.28), channel_id=1, source_target_pairs={{0,2},{2,4},{4,6},{6,8},{8,10},{10,12},{12,14},{1,3},{3,5},{5,7},{... | collective-permute-start | bytes 786440 | tf_op jit(solution)/shard_map/ppermute | solution.py:17
  258.0 3.4 %copy-start = (bf16[1024,9,212]{0,2,1:T(8,128)(2,1)S(1)}, bf16[1024,9,212]{0,2,1:T(8,128)(2,1)}, u32[]{:S(2)}) copy-start(bf16[1024,9,212]{0,2,1:T(8,128)(2,1)} %all-gather.5.cloned.1.call-done) | copy-start | bytes 11722756
Sparse Core Ops, SparseCore 0:
  10.0 74.9 all-gather.4
  96.5 7.7 reduce-scatter.1
  106.7 10.2 all-gather.6
  120.7 10.1 all-gather.8
  134.6 10.1 all-gather.10
  148.9 109.0 all-reduce.3
where the time goes:
time: 276 us
  waiting for transfers between devices  175 us (63%)
  blocking collectives  26.4 us (10%)
  matrix products  19.4 us (7%)
  local copies, waits for them, and re-layouts  17.9 us (6%)
  between operations  14.4 us (5%)
  starting transfers between devices  13.1 us (5%)
  other arithmetic  9.48 us (3%)
    psum x1, waiting for transfers between devices, per_device(): gamma_total, beta_total = lax.psum((gamma_terms, beta_terms), 'row')  89.7 us
    all_gather x1, waiting for transfers between devices, per_device(): shard_piece = lax.all_gather(conv_weight, 'row', axis=0, tiled=True)  60.2 us
    psum x1, blocking collectives, per_device(): gamma_total, beta_total = lax.psum((gamma_terms, beta_terms), 'row')  21.8 us
    ppermute x2, starting transfers between devices, extended(): before = lax.ppermute(last, axis, up)  10.2 us
    all_gather x1, waiting for transfers between devices, per_device(): squares = lax.all_gather(squares_own, 'chan', axis=0, tiled=True)  8.99 us
    reduce_scatter x1, waiting for transfers between devices, per_device(): lax.psum_scatter(partial_value, 'chan', scatter_dimension=0, tiled=True)  7.88 us
    dot_general x1, matrix products, per_device(): partial_value = jnp.dot(flat, columns, preferred_element_type=jnp.float32)  5.78 us
    reshape x1, local copies, waits for them, and re-layouts, per_device(): flat = shard_piece.reshape(shard_piece.shape[0], 9 * in_local)  5.54 us
  transfers between devices with their start and end apart: 10, of which 7 were waited for; matrix products, arithmetic and copies ran while one was open for 7% of the time, Pallas kernels for 0%

commit v1 on v0

--- a/solution.py
+++ b/solution.py
@@ -5,6 +5,18 @@
 from jax.sharding import PartitionSpec as P
 
 TAPS = ((-1, -1), (-1, 0), (-1, 1), (0, -1), (0, 0), (0, 1), (1, -1), (1, 0), (1, 1))
+
+
+def doubled_up(x, axis, dim):
+    ways, here = (lax.axis_size(axis), lax.axis_index(axis))
+    grown, reach = (x, 1)
+    while reach < ways:
+        theirs = lax.ppermute(grown, axis, [(d, d ^ reach) for d in range(ways)])
+        mine_first = jnp.concatenate([grown, theirs], axis=dim)
+        theirs_first = jnp.concatenate([theirs, grown], axis=dim)
+        grown = jnp.where(here & reach == 0, mine_first, theirs_first)
+        reach = 2 * reach
+    return grown
 
 
 def extended(shard, sides, width):
@@ -44,7 +56,7 @@
     lat_local = gdn_gamma.shape[0]
     rimmed = extended(band_strip, (("row", 1),), 1)
     columns = tap_columns(rimmed, row_count, col_count)
-    shard_piece = lax.all_gather(conv_weight, "row", axis=0, tiled=True)
+    shard_piece = doubled_up(conv_weight, "row", 0)
     flat = shard_piece.reshape(shard_piece.shape[0], 9 * in_local)
     partial_value = jnp.dot(flat, columns, preferred_element_type=jnp.float32)
     pre = lax.psum_scatter(partial_value, "chan", scatter_dimension=0, tiled=True)

time: 276 us -> 408 us (1.48)
  waiting for transfers between devices: 175 us -> 269 us
  other arithmetic: 9.48 us -> 24.6 us
  local copies, waits for them, and re-layouts: 17.9 us -> 27.5 us
  starting transfers between devices: 13.1 us -> 19.7 us
  matrix products: 19.4 us -> 24.1 us
    ppermute x0 -> x3, waiting for transfers between devices: none -> 96.6 us  [doubled_up(): theirs = lax.ppermute(grown, axis, [(d, d ^ reach) for d in range(ways)])]
    select_n x0 -> x4, other arithmetic: none -> 8.17 us  [doubled_up(): grown = jnp.where(here & reach == 0, mine_first, theirs_first)]
    ppermute x0 -> x3, starting transfers between devices: none -> 7.48 us  [doubled_up(): theirs = lax.ppermute(grown, axis, [(d, d ^ reach) for d in range(ways)])]
    concatenate x3, other arithmetic: 2.73 us -> 9.73 us  [extended(): shard = jnp.concatenate([before, shard, after], axis=dim)]
    concatenate x0 -> x4, local copies, waits for them, and re-layouts: none -> 6.07 us  [doubled_up(): mine_first = jnp.concatenate([grown, theirs], axis=dim)]
  transfers between devices with their start and end apart: 10 -> 13, of which waited for: 7 -> 9; matrix products, arithmetic and copies ran while one was open for 7% -> 10% of each run, Pallas kernels for 0% -> 0%
where the time goes in v1:
time: 408 us; the launch traced here: 407 us
  waiting for transfers between devices  269 us (66%)
  blocking collectives  28.4 us (7%)
  local copies, waits for them, and re-layouts  27.5 us (7%)
  other arithmetic  24.6 us (6%)
  matrix products  24.1 us (6%)
  starting transfers between devices  19.7 us (5%)
  between operations  14.4 us (4%)
    ppermute x3, waiting for transfers between devices, doubled_up(): theirs = lax.ppermute(grown, axis, [(d, d ^ reach) for d in range(ways)])  96.6 us
    psum x1, waiting for transfers between devices, per_device(): gamma_total, beta_total = lax.psum((gamma_terms, beta_terms), 'row')  92.2 us
    all_gather x1, waiting for transfers between devices, per_device(): shard_piece = lax.all_gather(conv_weight, 'row', axis=0, tiled=True)  56.8 us
    psum x1, blocking collectives, per_device(): gamma_total, beta_total = lax.psum((gamma_terms, beta_terms), 'row')  21.8 us
    reduce_scatter x1, waiting for transfers between devices, per_device(): lax.psum_scatter(partial_value, 'chan', scatter_dimension=0, tiled=True)  10.8 us
    all_gather x1, waiting for transfers between devices, per_device(): squares = lax.all_gather(squares_own, 'chan', axis=0, tiled=True)  10.2 us
    concatenate x3, other arithmetic, extended(): shard = jnp.concatenate([before, shard, after], axis=dim)  9.73 us
    ppermute x2, starting transfers between devices, extended(): before = lax.ppermute(last, axis, up)  9.26 us
  transfers between devices with their start and end apart: 13, of which 9 were waited for; matrix products, arithmetic and copies ran while one was open for 10% of the time, Pallas kernels for 0%

profile of v1, /device:TPU:0, one launch (start us, length us, event | category | flops | bytes accessed | tf_op | source)
XLA Modules:
  0.0 407.5 jit_solution(10096581388426115018)
XLA Ops:
  7.2 3.0 collective-permute-start
  10.3 11.6 %collective-permute-done = bf16[128,9,212]{0,2,1:T(8,128)(2,1)S(1)} collective-permute-done((bf16[128,9,212]{0,2,1:T(8,128)(2,1)}, bf16[128,9,212]{0,2,1:T(8,128)(2,1)S(1)}, u32[]{:S(2)}, u32[]{:S(2)}) %collective-permute-start) | collective-permute-done | bytes 488480 | tf_op jit(solution)/shard_map/ppermute | solution.py:14
  21.8 1.5 maximum_select_fusion.4
  23.3 1.9 collective-permute-start.1
  25.2 0.8 fusion.59
  26.0 1.3 collective-permute-start.4
  27.3 4.6 %collective-permute-start.3 = (bf16[212,1,128]{2,1,0:T(2,128)(2,1)S(1)}, bf16[212,1,128]{2,1,0:T(2,128)(2,1)S(1)}, u32[]{:S(2)}, u32[]{:S(2)}) collective-permute-start(bf16[212,1,128]{2,1,0:T(2,128)(2,1)S(1)} %get-tuple-element.18), channel_id=1, source_target_pairs={{0,2},{2,4},{4,6},{6,8},{8,10},{10,12},{12,14},{1,3},{3,5},{5,7},{... | collective-permute-start | bytes 162824 | tf_op jit(solution)/shard_map/ppermute | solution.py:29
  31.9 0.9 concatenate.58
  32.8 1.3 collective-permute-done.3
  34.2 1.1 fusion.44
  35.4 0.3 fusion.53
  35.6 12.1 %collective-permute-done.1 = bf16[256,9,212]{0,2,1:T(8,128)(2,1)S(1)} collective-permute-done((bf16[256,9,212]{0,2,1:T(8,128)(2,1)S(1)}, bf16[256,9,212]{0,2,1:T(8,128)(2,1)S(1)}, u32[]{:S(2)}, u32[]{:S(2)}) %collective-permute-start.1) | collective-permute-done | bytes 976928 | tf_op jit(solution)/shard_map/ppermute | solution.py:14
  47.7 1.9 maximum_select_fusion.2
  49.6 2.6 collective-permute-start.2
  52.2 0.3 fusion.51
  52.4 0.1 fusion.50
  52.7 0.4 fusion.49
  53.2 0.3 fusion.47
  53.5 0.4 fusion.45
  53.8 0.8 pad.58
  54.7 1.6 copy.23
  56.3 0.9 concatenate.59
  57.1 1.5 maximum_select_fusion.5
  58.6 1.1 concatenate.64
  59.7 3.4 maximum_select_fusion.3
  63.1 72.9 %collective-permute-done.2 = bf16[512,9,212]{0,2,1:T(8,128)(2,1)} collective-permute-done((bf16[512,9,212]{0,2,1:T(8,128)(2,1)}, bf16[512,9,212]{0,2,1:T(8,128)(2,1)}, u32[]{:S(2)}, u32[]{:S(2)}) %collective-permute-start.2) | collective-permute-done | bytes 1953824 | tf_op jit(solution)/shard_map/ppermute | solution.py:14
  136.0 3.2 concatenate.69
  139.2 7.0 %fusion.6 = f32[1024,512]{1,0:T(8,128)} fusion(bf16[1908,512]{1,0:T(8,128)(2,1)S(1)} %bitcast.146, bf16[512,1908]{0,1:T(8,128)(2,1)} %concatenate.69, bf16[512,1908]{0,1:T(8,128)(2,1)} %maximum_select_fusion.3, pred[]{:T(512)S(6)} %eq.9), kind=kOutput, calls=%fused_computation.9 | convolution fusion | flops 2018267136 | bytes 7958529 | tf_op jit(solution)/shard_map/dot_general | solution.py:61
  146.3 10.8 %reduce-scatter.2.cloned.1.call-done = f32[512,512]{1,0:T(8,128)} async-done(((f32[1024,512]{1,0:T(8,128)}), f32[512,512]{1,0:T(8,128)}) %reduce-scatter.2.cloned.1.call-update) | async-done | bytes 1048592 | tf_op jit(solution)/shard_map/reduce_scatter | solution.py:62
  157.1 2.2 multiply_convert_fusion.1
  159.6 10.2 %all-gather.5.cloned.1.call-done = bf16[1024,512]{1,0:T(8,128)(2,1)} async-done(((bf16[512,512]{1,0:T(8,128)(2,1)}), bf16[1024,512]{1,0:T(8,128)(2,1)}) %all-gather.5.cloned.1.call-update) | async-done | bytes 1048592 | tf_op jit(solution)/shard_map/all_gather | solution.py:64
  169.8 3.2 convert_reduce_fusion
  173.1 2.3 copy.18
  175.4 6.6 %all_to_all.19 = bf16[512,2,512]{0,2,1:T(8,128)(2,1)} all-to-all(bf16[512,2,512]{0,2,1:T(8,128)(2,1)} %bitcast.144), channel_id=1, replica_groups=mesh['grp'=2,'row'=8,'chan'=2] {'chan'}, dimensions={1} | all-to-all | bytes 2097152 | tf_op jit(solution)/shard_map/all_to_all | solution.py:70
  182.0 2.3 copy.19
  184.2 3.4 fusion.38
  187.6 2.1 reshape.69
  189.8 0.2 all-reduce.4.cloned.1.call-start
  190.0 3.1 fusion.60
  193.2 0.5 all-gather.11.cloned.1.call-update
  193.7 21.8 %psum.15 = f32[512]{0:T(512)S(1)} all-reduce(f32[512]{0:T(512)S(1)} %get-tuple-element.4), channel_id=1, replica_groups=mesh['grp'=2,'row'=8,'chan'=2] {'row'}, use_global_device_ids=true, to_apply=%region_3.4 | all-reduce | flops 512 | bytes 4096 | tf_op jit(solution)/shard_map/psum | solution.py:80
  215.5 0.6 broadcast_multiply_fusion.1
  216.1 0.9 reshape.68
  217.0 2.6 fusion.58
  219.7 1.3 collective-permute-start.6
  221.0 4.7 %collective-permute-start.5 = (bf16[1024,1,128]{2,1,0:T(2,128)(2,1)S(1)}, bf16[1024,1,128]{2,1,0:T(2,128)(2,1)S(1)}, u32[]{:S(2)}, u32[]{:S(2)}) collective-permute-start(bf16[1024,1,128]{2,1,0:T(2,128)(2,1)S(1)} %get-tuple-element.16), channel_id=1, source_target_pairs={{0,2},{2,4},{4,6},{6,8},{8,10},{10,12},{12,14},{1,3},{3,5},{5,7},{... | collective-permute-start | bytes 786440 | tf_op jit(solution)/shard_map/ppermute | solution.py:29
  225.7 92.2 %all-reduce.4.cloned.1.call-done = f32[512,1024]{1,0:T(8,128)} async-done(((f32[512,1024]{1,0:T(8,128)}), f32[512,1024]{1,0:T(8,128)}) %all-reduce.4.cloned.1.call-update) | async-done | bytes 2097168 | tf_op jit(solution)/shard_map/psum | solution.py:80
  317.9 3.2 broadcast_multiply_fusion
  321.1 3.3 pad_maximum_fusion
  324.5 5.3 %fusion.5 = bf16[1024,6,130]{2,1,0:T(8,128)(2,1)S(1)} fusion(bf16[1024,1,128]{2,1,0:T(2,128)(2,1)S(1)} %collective-permute-done.6, bf16[1024,4,128]{2,1,0:T(4,128)(2,1)S(1)} %copy-done.1, bf16[1024,1,128]{2,1,0:T(2,128)(2,1)S(1)} %collective-permute-done.5), kind=kLoop, calls=%fused_computation.7 | loop fusion | flops 9584640 | bytes 3170304 | tf_op jit(solution)/shard_map/concatenate | solution.py:31
  329.8 4.8 %fusion.57 = (bf16[1024,4,128]{2,1,0:T(4,128)(2,1)S(1)}, bf16[1024,4,128]{2,1,0:T(4,128)(2,1)S(1)}, bf16[1024,4,128]{2,1,0:T(4,128)(2,1)}, bf16[1024,4,128]{2,1,...) fusion(bf16[1024,6,130]{2,1,0:T(8,128)(2,1)S(1)} %fusion.5), kind=kLoop, calls=%fused_computation.103 | loop fusion | bytes 12582912 | tf_op jit(solution)/shard_map/slice | solution.py:94
  334.6 56.8 %all-gather.11.cloned.1.call-done = bf16[1024,9,212]{0,2,1:T(8,128)(2,1)} async-done(((bf16[128,9,212]{0,2,1:T(8,128)(2,1)}), bf16[1024,9,212]{0,2,1:T(8,128)(2,1)}) %all-gather.11.cloned.1.call-update) | async-done | bytes 3907600 | tf_op jit(solution)/shard_map/all_gather | solution.py:91
  391.4 1.9 fusion.34
  393.3 1.7 convolution_add_fusion.8
  395.0 1.4 convolution_add_fusion.7
  396.5 0.4 convolution_add_fusion.6
  396.9 0.4 convolution_add_fusion.5
  397.3 0.4 copy-done.8
  397.7 0.4 convolution_add_fusion.4
  398.1 0.4 convolution_add_fusion.3
  398.5 0.4 copy-done.11
  398.9 0.4 convolution_add_fusion.2
  399.3 0.4 fusion.16
  399.7 0.9 reshape.79
  (49 shorter events, 0.9 us)
Async XLA Ops:
  7.2 24.7 %copy-start.3 = (bf16[128,9,212]{0,2,1:T(8,128)(2,1)S(1)}, bf16[128,9,212]{0,2,1:T(8,128)(2,1)}, u32[]{:S(2)}) copy-start(bf16[128,9,212]{0,2,1:T(8,128)(2,1)} %param.6) | copy-start | bytes 1465348
  7.2 18.0 %copy-start.2 = (bf16[212,4,128]{2,1,0:T(4,128)(2,1)S(1)}, bf16[212,4,128]{2,1,0:T(4,128)(2,1)}, u32[]{:S(2)}) copy-start(bf16[212,4,128]{2,1,0:T(4,128)(2,1)} %param.5) | copy-start | bytes 651268
  7.2 150.0 %reduce-scatter.2.cloned.1.call-start = ((), (), s32[]{:S(2)}) async-start(), calls=%async_computation.2 | async-start | bytes 3145728 | tf_op jit(solution)/shard_map/reduce_scatter | solution.py:62
  7.2 14.6 %collective-permute-start = (bf16[128,9,212]{0,2,1:T(8,128)(2,1)}, bf16[128,9,212]{0,2,1:T(8,128)(2,1)S(1)}, u32[]{:S(2)}, u32[]{:S(2)}) collective-permute-start(bf16[128,9,212]{0,2,1:T(8,128)(2,1)} %param.6), channel_id=1, source_target_pairs={{0,2},{2,0},{4,6},{6,4},{8,10},{10,8},{12,14},{14,12},{1,3},{3,1},... | collective-permute-start | bytes 1465352 | tf_op jit(solution)/shard_map/ppermute | solution.py:14
  23.3 24.4 %collective-permute-start.1 = (bf16[256,9,212]{0,2,1:T(8,128)(2,1)S(1)}, bf16[256,9,212]{0,2,1:T(8,128)(2,1)S(1)}, u32[]{:S(2)}, u32[]{:S(2)}) collective-permute-start(bf16[256,9,212]{0,2,1:T(8,128)(2,1)S(1)} %maximum_select_fusion.4), channel_id=1, source_target_pairs={{0,4},{2,6},{4,0},{6,2},{8,12},{10,14},{12,8},{14,10},{1,5},{3,7},... | collective-permute-start | bytes 2930696 | tf_op jit(solution)/shard_map/ppermute | solution.py:14
  26.0 6.8 %collective-permute-start.4 = (bf16[212,1,128]{2,1,0:T(2,128)(2,1)}, bf16[212,1,128]{2,1,0:T(2,128)(2,1)S(1)}, u32[]{:S(2)}, u32[]{:S(2)}) collective-permute-start(bf16[212,1,128]{2,1,0:T(2,128)(2,1)} %get-tuple-element.19), channel_id=1, source_target_pairs={{2,0},{4,2},{6,4},{8,6},{10,8},{12,10},{14,12},{3,1},{5,3},{7,5},{... | collective-permute-start | bytes 162824 | tf_op jit(solution)/shard_map/ppermute | solution.py:30
  27.3 6.8 %collective-permute-start.3 = (bf16[212,1,128]{2,1,0:T(2,128)(2,1)S(1)}, bf16[212,1,128]{2,1,0:T(2,128)(2,1)S(1)}, u32[]{:S(2)}, u32[]{:S(2)}) collective-permute-start(bf16[212,1,128]{2,1,0:T(2,128)(2,1)S(1)} %get-tuple-element.18), channel_id=1, source_target_pairs={{0,2},{2,4},{4,6},{6,8},{8,10},{10,12},{12,14},{1,3},{3,5},{5,7},{... | collective-permute-start | bytes 162824 | tf_op jit(solution)/shard_map/ppermute | solution.py:29
  49.6 86.4 %collective-permute-start.2 = (bf16[512,9,212]{0,2,1:T(8,128)(2,1)}, bf16[512,9,212]{0,2,1:T(8,128)(2,1)}, u32[]{:S(2)}, u32[]{:S(2)}) collective-permute-start(bf16[512,9,212]{0,2,1:T(8,128)(2,1)} %maximum_select_fusion.2), channel_id=1, source_target_pairs={{0,8},{2,10},{4,12},{6,14},{8,0},{10,2},{12,4},{14,6},{1,9},{3,11}... | collective-permute-start | bytes 5861384 | tf_op jit(solution)/shard_map/ppermute | solution.py:14
  54.7 2.5 copy-start.7
  63.1 76.1 %copy-start.6 = (bf16[239,8,4,128]{3,1,2,0:T(8,128)(2,1)S(1)}, bf16[239,8,4,128]{3,1,2,0:T(8,128)(2,1)}, u32[]{:S(2)}) copy-start(bf16[239,8,4,128]{3,1,2,0:T(8,128)(2,1)} %copy.23) | copy-start | bytes 5873668
  146.2 13.2 %copy-start.13 = (bf16[512,4,128]{2,1,0:T(4,128)(2,1)S(1)}, bf16[512,4,128]{2,1,0:T(4,128)(2,1)}, u32[]{:S(2)}) copy-start(bf16[512,4,128]{2,1,0:T(4,128)(2,1)} %param.9) | copy-start | bytes 1572868
  146.3 23.6 %copy-start.14 = (f32[512]{0:T(512)S(1)}, f32[512]{0:T(512)}, u32[]{:S(2)}) copy-start(f32[512]{0:T(512)} %param.8) | copy-start | bytes 6148
  146.3 23.5 %all-gather.5.cloned.1.call-start = ((), (), s32[]{:S(2)}) async-start(), calls=%async_computation.3 | async-start | bytes 1572864 | tf_op jit(solution)/shard_map/all_gather | solution.py:64
  157.1 12.7 %copy-start = (f32[512,512]{1,0:T(8,128)S(1)}, f32[512,512]{1,0:T(8,128)}, u32[]{:S(2)}) copy-start(f32[512,512]{1,0:T(8,128)} %reduce-scatter.2.cloned.1.call-done) | copy-start | bytes 3145732
  159.4 24.9 %all-gather.7.cloned.1.call-start = ((), (), s32[]{:S(2)}) async-start(), calls=%async_computation.4 | async-start | bytes 1572864 | tf_op jit(solution)/shard_map/all_gather | solution.py:71
  173.0 44.0 %all-gather.9.cloned.1.call-start = ((), (), s32[]{:S(2)}) async-start(), calls=%async_computation.5 | async-start | bytes 1572864 | tf_op jit(solution)/shard_map/all_gather | solution.py:84
  187.6 2.4 copy-start.4
  189.8 128.2 %all-reduce.4.cloned.1.call-start = ((), (), s32[]{:S(2)}) async-start(), calls=%async_computation.7 | async-start | bytes 4194304 | tf_op jit(solution)/shard_map/psum | solution.py:80
  193.1 23.0 %copy-start.5 = (bf16[512,512]{1,0:T(8,128)(2,1)S(1)}, bf16[512,512]{1,0:T(8,128)(2,1)}, u32[]{:S(2)}) copy-start(bf16[512,512]{1,0:T(8,128)(2,1)} %get-tuple-element.13) | copy-start | bytes 1572868
  193.1 198.2 %all-gather.11.cloned.1.call-start = ((), (), s32[]{:S(2)}) async-start(), calls=%async_computation.6 | async-start | bytes 4478976 | tf_op jit(solution)/shard_map/all_gather | solution.py:91
  219.7 101.5 %collective-permute-start.6 = (bf16[1024,1,128]{2,1,0:T(2,128)(2,1)S(1)}, bf16[1024,1,128]{2,1,0:T(2,128)(2,1)S(1)}, u32[]{:S(2)}, u32[]{:S(2)}) collective-permute-start(bf16[1024,1,128]{2,1,0:T(2,128)(2,1)S(1)} %get-tuple-element.17), channel_id=1, source_target_pairs={{2,0},{4,2},{6,4},{8,6},{10,8},{12,10},{14,12},{3,1},{5,3},{7,5},{... | collective-permute-start | bytes 786440 | tf_op jit(solution)/shard_map/ppermute | solution.py:30
  221.0 100.2 %copy-start.1 = (bf16[1024,4,128]{2,1,0:T(4,128)(2,1)S(1)}, bf16[1024,4,128]{2,1,0:T(4,128)(2,1)}, u32[]{:S(2)}) copy-start(bf16[1024,4,128]{2,1,0:T(4,128)(2,1)} %all-gather.9.cloned.1.call-done) | copy-start | bytes 3145732
  221.0 100.2 %collective-permute-start.5 = (bf16[1024,1,128]{2,1,0:T(2,128)(2,1)S(1)}, bf16[1024,1,128]{2,1,0:T(2,128)(2,1)S(1)}, u32[]{:S(2)}, u32[]{:S(2)}) collective-permute-start(bf16[1024,1,128]{2,1,0:T(2,128)(2,1)S(1)} %get-tuple-element.16), channel_id=1, source_target_pairs={{0,2},{2,4},{4,6},{6,8},{8,10},{10,12},{12,14},{1,3},{3,5},{5,7},{... | collective-permute-start | bytes 786440 | tf_op jit(solution)/shard_map/ppermute | solution.py:29
  391.3 1.9 copy-start.12
  391.3 3.7 copy-start.10
  391.4 5.1 %copy-start.15 = (bf16[1024,9,212]{0,2,1:T(8,128)(2,1)S(1)}, bf16[1024,9,212]{0,2,1:T(8,128)(2,1)}, u32[]{:S(2)}) copy-start(bf16[1024,9,212]{0,2,1:T(8,128)(2,1)} %all-gather.11.cloned.1.call-done) | copy-start | bytes 11722756
  393.2 3.2 copy-start.9
  396.5 1.2 copy-start.8
  397.7 1.2 copy-start.11
Sparse Core Ops, SparseCore 0:
  146.4 10.7 reduce-scatter.1
  159.5 10.2 all-gather.4
  173.2 10.1 all-gather.6
  189.9 10.1 all-gather.8
  204.1 113.7 all-reduce.3
  319.8 71.4 all-gather.10
